TPU v7x, 512 devices: a whole 4x4x16 slice. The times are simulated.
512 devices in a mesh: tm: 64 (over z, y), area: 8 (over x, core).
Axes of the slice: x: 4, y: 4, z: 16, core: 2. Of those that a mesh axis runs over, the one named last changes fastest.
Arguments:
- demand: float32 [256, 71680], P('tm', 'area'), may hold values from -6 to 6
- unit_cost: float32 [256, 65536], P('tm', 'area'), may hold values from -18 to 18
- ptdf_tiles: bfloat16 [192, 128, 256], P('area'), may hold values from -0.25 to 0.25
- tile_area: int32 [192, 1], replicated, may hold values from 0 to 7; in each aligned block of 24 rows (0 to 23, 24 to 47, ...) at most 6 rows name the same one
- tile_block: int32 [192], replicated, may hold values from 0 to 34
- tile_row: int32 [192], replicated, may hold values from 0 to 11
- unit_bus: int32 [65536], P('area'), may hold values from 0 to 8959
- unit_class: int32 [65536], P('area'), may hold values from 0 to 2
- power_cap: float32 [65536], P('area'), may hold values from 0.1 to 2
- line_limit: float32 [12288], P('area'), may hold values from 0.2 to 2
- smoother: float32 [3, 256], replicated, as said below
Outputs:
- power: float32 [256, 65536], P('tm', 'area')
- line_duals: float32 [256, 12288], P('tm', 'area')
- primal_rms: float32 [2], replicated
Inputs may be any that keep to these rules, and one draw needn't show every extreme that they name: `tile_area`: among the 24 tiles of one holder, at most 6 have their column block in one area, and some holder reaches 6. `smoother`: row k is the first column of the inverse of (c1 I + L)(c2 I + L) / (c1 c2) of order 256, with L = 2 I - S - S^T the cyclic second difference and class constants 1e-5 <= c1 < c2 <= 1.
All inputs are finite; a program needn't handle non-finite values.
Results may differ from a plain program's by a relative error of at most 0.0028.
Values may be sent and summed in bfloat16 or wider, within the bound.
No kernel may reach another device: no remote copies, remote signals or barrier semaphores. Data moves between devices by JAX's collectives and lax.ppermute only.
A program may use at most 64 MiB of HBM per device.

v0:
```python
import functools
import math
import jax
import jax.numpy as jnp
from jax import lax
from jax.sharding import Mesh
from jax.sharding import PartitionSpec as P

ITERATIONS = 2
TM = ("tm_0", "tm_1")
AREA = ("area_0", "area_1")
TM_AREA = ("tm_0", "tm_1", "area_0", "area_1")
step_size = 0.5
rho_weight = 1.0


def laid_out(tiles, dim):
    dims = list(tiles.shape[1:])
    dims[dim] *= tiles.shape[0]
    return jnp.moveaxis(tiles, 0, dim).reshape(dims)


def copy_for_each(array, axis):
    count = lax.axis_size(axis)
    return lax.all_to_all(
        jnp.broadcast_to(array[None], (count, *array.shape)), axis, 0, 0, tiled=True
    )


def collect(array, axis, dim):
    return laid_out(copy_for_each(array, axis), dim)


def one_axis_at_a_time(array, axes):
    return functools.reduce(lax.psum, axes, array)


def per_device(
    demand,
    unit_cost,
    ptdf_tiles,
    tile_area,
    tile_block,
    tile_row,
    unit_bus,
    unit_class,
    power_cap,
    line_limit,
    smoother,
):
    time_devices = lax.axis_size(TM)
    area_devices = lax.axis_size(AREA)
    block_steps, bus_area = demand.shape
    unit_area = unit_cost.shape[1]
    tile_count, line_block, panel_width = ptdf_tiles.shape
    col_blocks = bus_area // panel_width
    row_blocks = line_limit.shape[0] // line_block
    capacity = 2 * tile_count // area_devices
    horizon = block_steps * time_devices
    unit_width = unit_area // time_devices
    area_index = lax.axis_index(AREA)
    time_index = lax.axis_index(TM)
    tile_areas = tile_area.reshape(area_devices, tile_count)
    block_grid = tile_block.reshape(area_devices, tile_count)
    row_grid = tile_row.reshape(area_devices, tile_count)
    is_source = (tile_areas == area_index).astype(jnp.int32)
    rank_source = jnp.cumsum(is_source, axis=1) - 1
    slot_ids = jnp.arange(capacity, dtype=jnp.int32)
    chosen = is_source[:, None, :] * (rank_source[:, None, :] == slot_ids[None, :, None]).astype(
        jnp.int32
    )
    send_block = jnp.sum(chosen * block_grid[:, None, :], axis=2).reshape(-1)
    my_areas = lax.dynamic_index_in_dim(tile_areas, area_index, 0, keepdims=False)
    my_blocks = lax.dynamic_index_in_dim(block_grid, area_index, 0, keepdims=False)
    my_rows = lax.dynamic_index_in_dim(row_grid, area_index, 0, keepdims=False)
    positions = jnp.arange(tile_count, dtype=jnp.int32)
    earlier = positions[None, :] <= positions[:, None]
    same_area = my_areas[None, :] == my_areas[:, None]
    rank_mine = jnp.sum((same_area & earlier).astype(jnp.int32), axis=1) - 1
    slot_of_tile = my_areas * capacity + rank_mine
    my_columns = my_areas * col_blocks + my_blocks
    my_class = lax.dynamic_slice_in_dim(unit_class, time_index * unit_width, unit_width)
    my_cap = lax.dynamic_slice_in_dim(power_cap, time_index * unit_width, unit_width)
    half_steps = horizon // 2
    steps_line = jnp.arange(horizon, dtype=jnp.int32)
    frequency = jnp.concatenate(
        [jnp.arange(half_steps + 1, dtype=jnp.int32), jnp.arange(1, half_steps, dtype=jnp.int32)]
    )
    angle = (frequency[:, None] * steps_line[None, :] % horizon).astype(jnp.float32) * (
        2.0 * math.pi / horizon
    )
    cosine_rows = (steps_line <= half_steps)[:, None]
    forward = jnp.where(cosine_rows, jnp.cos(angle), -jnp.sin(angle))
    edge_rows = (frequency == 0) | (frequency == half_steps)
    row_weight = (jnp.where(edge_rows, 1.0, 2.0).astype(jnp.float32) / horizon)[:, None]
    kernel_spectrum = jnp.dot(
        forward, smoother.T, precision=lax.Precision.HIGHEST, preferred_element_type=jnp.float32
    )
    class_table = (
        my_class[None, :] == jnp.arange(smoother.shape[0], dtype=jnp.int32)[:, None]
    ).astype(jnp.float32)
    unit_spectrum = jnp.dot(
        kernel_spectrum,
        class_table,
        precision=lax.Precision.HIGHEST,
        preferred_element_type=jnp.float32,
    )
    empty_row = jnp.zeros((1, unit_width), jnp.float32)
    kernel_real = unit_spectrum[: half_steps + 1]
    kernel_imag = jnp.concatenate([empty_row, unit_spectrum[half_steps + 1 :], empty_row], axis=0)
    power_time = jnp.zeros((block_steps, unit_area), jnp.float32)
    line_duals = jnp.zeros((block_steps, line_limit.shape[0]), jnp.float32)
    totals = []
    for repeat in range(ITERATIONS):
        if repeat == 0:
            injection = demand.astype(jnp.bfloat16)
        else:
            injection = demand.at[:, unit_bus].add(power_time).astype(jnp.bfloat16)
        gathered = collect(injection, AREA, 1)
        panels = jnp.take(
            gathered.reshape(block_steps, area_devices * col_blocks, panel_width),
            my_columns,
            axis=1,
        )
        partial_value = jnp.einsum(
            "tjb,jlb->tjl", panels, ptdf_tiles, preferred_element_type=jnp.float32
        )
        line_flows = (
            jnp.zeros((block_steps, row_blocks, line_block), jnp.float32)
            .at[:, my_rows]
            .add(partial_value)
        )
        line_flows = line_flows.reshape(block_steps, row_blocks * line_block)
        limits = line_limit[None, :]
        clipped = jnp.clip(line_flows + line_duals, -limits, limits)
        line_duals = line_duals + line_flows - clipped
        excess = line_flows - clipped
        local_total = jnp.sum(excess * excess)
        totals.append(local_total)
        weights = (line_duals + line_flows - clipped).astype(jnp.bfloat16)
        picked = jnp.take(weights.reshape(block_steps, row_blocks, line_block), my_rows, axis=1)
        contrib = jnp.einsum("tjl,jlb->tjb", picked, ptdf_tiles, preferred_element_type=jnp.float32)
        outbound = (
            jnp.zeros((block_steps, area_devices * capacity, panel_width), jnp.float32)
            .at[:, slot_of_tile]
            .set(contrib)
        )
        outbound = outbound.reshape(block_steps, area_devices, capacity, panel_width)
        returned = lax.all_to_all(outbound, AREA, split_axis=1, concat_axis=1, tiled=True)
        prices = (
            jnp.zeros((block_steps, col_blocks, panel_width), jnp.float32)
            .at[:, send_block]
            .add(returned.reshape(block_steps, area_devices * capacity, panel_width))
        )
        prices = prices.reshape(block_steps, bus_area)
        gradient = unit_cost + rho_weight * jnp.take(prices, unit_bus, axis=1)
        target = power_time - step_size * gradient
        columns = lax.all_to_all(target, TM, split_axis=1, concat_axis=0, tiled=True)
        spectrum = jnp.dot(
            forward, columns, precision=lax.Precision.HIGHEST, preferred_element_type=jnp.float32
        )
        spectrum_real = spectrum[: half_steps + 1]
        spectrum_imag = jnp.concatenate([empty_row, spectrum[half_steps + 1 :], empty_row], axis=0)
        product_real = spectrum_real * kernel_real - spectrum_imag * kernel_imag
        product_imag = spectrum_real * kernel_imag + spectrum_imag * kernel_real
        stacked = jnp.concatenate([product_real, product_imag[1:half_steps]], axis=0) * row_weight
        smoothed = lax.dot_general(
            forward,
            stacked,
            (((0,), (0,)), ((), ())),
            precision=lax.Precision.HIGHEST,
            preferred_element_type=jnp.float32,
        )
        power_cols = jnp.clip(smoothed, -my_cap[None, :], my_cap[None, :])
        power_time = lax.all_to_all(power_cols, TM, split_axis=0, concat_axis=1, tiled=True)
    entries = float(horizon * line_limit.shape[0] * area_devices)
    summed = lax.psum(jnp.stack(totals), TM_AREA)
    primal_rms = jnp.sqrt(summed / entries)
    return (power_time, line_duals, primal_rms)


def solution(mesh):
    finer = Mesh(mesh.devices.reshape(16, 4, 4, 2), ("tm_0", "tm_1", "area_0", "area_1"))
    placed = (
        P(TM, AREA),
        P(TM, AREA),
        P(AREA, None, None),
        P(),
        P(),
        P(),
        P(AREA),
        P(AREA),
        P(AREA),
        P(AREA),
        P(),
    )
    return jax.shard_map(
        per_device,
        mesh=finer,
        in_specs=placed,
        out_specs=(P(TM, AREA), P(TM, AREA), P()),
        check_vma=False,
    )
```

profile of v0, /device:TPU:8, one launch (start us, length us, event | category | flops | bytes accessed | tf_op | source)
XLA Modules:
  0.0 396.6 jit_solution(17762997398970816326)
XLA Ops:
  2.7 4.3 %all-to-all-start = ((bf16[8,4,8960]{2,1,0:T(4,128)(2,1)}), bf16[8,4,8960]{2,1,0:T(4,128)(2,1)S(1)}, u32[]{:S(2)}, u32[]{:S(2)}) async-start(bf16[8,4,8960]{2,1,0:T(4,128)(2,1)} %broadcast_in_dim.55), calls=%async_computation | async-start | bytes 1146880 | tf_op jit(solution)/shard_map/all_to_all | solution.py:25
  14.3 3.5 all-to-all-done
  19.0 1.7 scatter_fusion
  22.4 3.7 scatter_fusion.1
  26.1 3.4 all-to-all-start.1
  29.5 6.7 %all-to-all-done.1 = f32[4,8,6,256]{3,0,2,1:T(4,128)S(1)} async-done(((f32[4,8,6,256]{3,0,2,1:T(4,128)}), f32[4,8,6,256]{3,0,2,1:T(4,128)S(1)}, u32[]{:S(2)}, u32[]{:S(2)}) %all-to-all-start.1) | async-done | bytes 196640 | tf_op jit(solution)/shard_map/all_to_all | solution.py:149
  36.2 2.4 scatter_fusion.2
  38.6 2.8 copy.80
  41.4 30.0 %gather_fusion.2 = f32[8192,4]{1,0:T(8,128)} fusion(f32[4,8960]{0,1:T(8,128)} %copy.80, s32[8192]{0:T(1024)S(1)} %get-tuple-element.26), kind=kCustom, calls=%fused_computation.2.clone | custom fusion | bytes 294912 | tf_op jit(solution)/shard_map/jit(_take)/gather | solution.py:156
  71.4 2.8 copy.81
  75.0 18.7 %all-to-all-start.2 = ((f32[4,64,128]{2,0,1:T(4,128)}), f32[4,64,128]{2,0,1:T(4,128)S(1)}, u32[]{:S(2)}, u32[]{:S(2)}) async-start(f32[4,64,128]{2,0,1:T(4,128)} %fusion.17), calls=%async_computation.2 | async-start | bytes 262144 | tf_op jit(solution)/shard_map/all_to_all | solution.py:158
  96.5 13.5 %all-to-all-done.2 = f32[4,64,128]{2,0,1:T(4,128)S(1)} async-done(((f32[4,64,128]{2,0,1:T(4,128)}), f32[4,64,128]{2,0,1:T(4,128)S(1)}, u32[]{:S(2)}, u32[]{:S(2)}) %all-to-all-start.2) | async-done | bytes 131104 | tf_op jit(solution)/shard_map/all_to_all | solution.py:158
  110.0 2.2 fusion.20
  112.3 2.3 fusion.1
  114.7 5.6 %all-to-all-start.3 = ((f32[64,4,128]{2,1,0:T(4,128)}), f32[64,4,128]{2,1,0:T(4,128)S(1)}, u32[]{:S(2)}, u32[]{:S(2)}) async-start(f32[64,4,128]{2,1,0:T(4,128)} %bitcast.23), calls=%async_computation.3 | async-start | bytes 262144 | tf_op jit(solution)/shard_map/all_to_all | solution.py:175
  120.3 2.8 copy.83
  123.1 12.8 %all-to-all-done.3 = f32[64,4,128]{2,1,0:T(4,128)S(1)} async-done(((f32[64,4,128]{2,1,0:T(4,128)}), f32[64,4,128]{2,1,0:T(4,128)S(1)}, u32[]{:S(2)}, u32[]{:S(2)}) %all-to-all-start.3) | async-done | bytes 131104 | tf_op jit(solution)/shard_map/all_to_all | solution.py:175
  135.9 2.7 copy.84
  138.6 44.2 %scatter_fusion.3 = f32[4,8960]{0,1:T(8,128)} fusion(f32[4,8960]{0,1:T(8,128)} %copy.83, s32[8192]{0:T(1024)S(1)} %get-tuple-element.25, f32[8192,4]{1,0:T(8,128)} %copy.84), kind=kCustom, calls=%fused_computation.9 | custom fusion | flops 32768 | bytes 425984 | tf_op jit(solution)/shard_map/scatter-add | solution.py:118
  182.8 3.0 copy.85
  186.0 13.3 %all_to_all.96 = bf16[8,4,8960]{2,1,0:T(4,128)(2,1)S(1)} all-to-all(bf16[8,4,8960]{2,1,0:T(4,128)(2,1)S(1)} %broadcast_in_dim.60), channel_id=1, replica_groups=mesh['tm_0'=16,'tm_1'=4,'area_0'=4,'area_1'=2] {'area_0','area_1'}, dimensions={0} | all-to-all | bytes 1146880 | tf_op jit(solution)/shard_map/all_to_all | solution.py:25
  205.3 9.2 %all_to_all.97 = f32[4,8,6,256]{3,0,2,1:T(4,128)S(1)} all-to-all(f32[4,8,6,256]{3,0,2,1:T(4,128)S(1)} %bitcast.125), channel_id=1, replica_groups=mesh['tm_0'=16,'tm_1'=4,'area_0'=4,'area_1'=2] {'area_0','area_1'}, dimensions={1} | all-to-all | bytes 393216 | tf_op jit(solution)/shard_map/all_to_all | solution.py:149
  214.5 2.4 scatter_fusion.6
  216.9 2.8 copy.88
  219.7 30.0 %gather_fusion.5 = f32[8192,4]{1,0:T(8,128)} fusion(f32[4,8960]{0,1:T(8,128)} %copy.88, s32[8192]{0:T(1024)S(1)} %get-tuple-element.26), kind=kCustom, calls=%fused_computation.5.clone | custom fusion | bytes 294912 | tf_op jit(solution)/shard_map/jit(_take)/gather | solution.py:156
  249.7 2.8 copy.89
  253.3 5.8 %all-to-all-start.6 = ((f32[4,64,128]{2,0,1:T(4,128)}), f32[4,64,128]{2,0,1:T(4,128)S(1)}, u32[]{:S(2)}, u32[]{:S(2)}) async-start(f32[4,64,128]{2,0,1:T(4,128)} %fusion.14), calls=%async_computation.6 | async-start | bytes 262144 | tf_op jit(solution)/shard_map/all_to_all | solution.py:158
  260.4 102.7 %psum.7 = f32[2]{0:T(128)S(1)} all-reduce(f32[2]{0:T(128)S(1)} %pad_maximum_fusion.6), channel_id=1, replica_groups=mesh['tm_0'=16,'tm_1'=4,'area_0'=4,'area_1'=2] {'tm_0','tm_1','area_0','..., use_global_device_ids=true, to_apply=%region_12.16 | all-reduce | flops 2 | bytes 16 | tf_op jit(solution)/shard_map/psum | solution.py:177
  363.1 2.2 fusion.18
  365.4 2.3 fusion
  367.8 11.6 %all-to-all-start.7 = ((f32[64,4,128]{2,1,0:T(4,128)}), f32[64,4,128]{2,1,0:T(4,128)S(1)}, u32[]{:S(2)}, u32[]{:S(2)}) async-start(f32[64,4,128]{2,1,0:T(4,128)} %bitcast.40), calls=%async_computation.7 | async-start | bytes 262144 | tf_op jit(solution)/shard_map/all_to_all | solution.py:175
  380.6 15.4 %all-to-all-done.7 = f32[64,4,128]{2,1,0:T(4,128)S(1)} async-done(((f32[64,4,128]{2,1,0:T(4,128)}), f32[64,4,128]{2,1,0:T(4,128)S(1)}, u32[]{:S(2)}, u32[]{:S(2)}) %all-to-all-start.7) | async-done | bytes 131104 | tf_op jit(solution)/shard_map/all_to_all | solution.py:175
  (76 shorter events, 26.0 us)
Async XLA Ops:
  0.6 17.8 %copy-start = (bf16[24,128,256]{2,1,0:T(8,128)(2,1)S(1)}, bf16[24,128,256]{2,1,0:T(8,128)(2,1)}, u32[]{:S(2)}) copy-start(bf16[24,128,256]{2,1,0:T(8,128)(2,1)} %param.19) | copy-start | bytes 4718596
  0.6 20.1 %copy-start.3 = (f32[1536]{0:T(1024)S(1)}, f32[1536]{0:T(1024)}, u32[]{:S(2)}) copy-start(f32[1536]{0:T(1024)} %param.26) | copy-start | bytes 18436
  2.7 15.1 %all-to-all-start = ((bf16[8,4,8960]{2,1,0:T(4,128)(2,1)}), bf16[8,4,8960]{2,1,0:T(4,128)(2,1)S(1)}, u32[]{:S(2)}, u32[]{:S(2)}) async-start(bf16[8,4,8960]{2,1,0:T(4,128)(2,1)} %broadcast_in_dim.55), calls=%async_computation | async-start | bytes 1146880 | tf_op jit(solution)/shard_map/all_to_all | solution.py:25
  26.1 10.1 %all-to-all-start.1 = ((f32[4,8,6,256]{3,0,2,1:T(4,128)}), f32[4,8,6,256]{3,0,2,1:T(4,128)S(1)}, u32[]{:S(2)}, u32[]{:S(2)}) async-start(f32[4,8,6,256]{3,0,2,1:T(4,128)} %bitcast.15), calls=%async_computation.1 | async-start | bytes 393216 | tf_op jit(solution)/shard_map/all_to_all | solution.py:149
  38.6 35.7 %copy-start.2 = (f32[4,8192]{1,0:T(4,128)S(1)}, f32[4,8192]{1,0:T(4,128)}, u32[]{:S(2)}) copy-start(f32[4,8192]{1,0:T(4,128)} %param.18) | copy-start | bytes 393220
  41.4 52.3 %copy-start.4 = (f32[3,256]{1,0:T(4,128)S(1)}, f32[3,256]{1,0:T(4,128)}, u32[]{:S(2)}) copy-start(f32[3,256]{1,0:T(4,128)} %param.27) | copy-start | bytes 9220
  74.3 46.0 %copy-start.1 = (f32[4,8960]{1,0:T(4,128)S(1)}, f32[4,8960]{1,0:T(4,128)}, u32[]{:S(2)}) copy-start(f32[4,8960]{1,0:T(4,128)} %param.17) | copy-start | bytes 430084
  75.0 35.0 %all-to-all-start.2 = ((f32[4,64,128]{2,0,1:T(4,128)}), f32[4,64,128]{2,0,1:T(4,128)S(1)}, u32[]{:S(2)}, u32[]{:S(2)}) async-start(f32[4,64,128]{2,0,1:T(4,128)} %fusion.17), calls=%async_computation.2 | async-start | bytes 262144 | tf_op jit(solution)/shard_map/all_to_all | solution.py:158
  114.7 21.2 %all-to-all-start.3 = ((f32[64,4,128]{2,1,0:T(4,128)}), f32[64,4,128]{2,1,0:T(4,128)S(1)}, u32[]{:S(2)}, u32[]{:S(2)}) async-start(f32[64,4,128]{2,1,0:T(4,128)} %bitcast.23), calls=%async_computation.3 | async-start | bytes 262144 | tf_op jit(solution)/shard_map/all_to_all | solution.py:175
  253.3 109.9 %all-to-all-start.6 = ((f32[4,64,128]{2,0,1:T(4,128)}), f32[4,64,128]{2,0,1:T(4,128)S(1)}, u32[]{:S(2)}, u32[]{:S(2)}) async-start(f32[4,64,128]{2,0,1:T(4,128)} %fusion.14), calls=%async_computation.6 | async-start | bytes 262144 | tf_op jit(solution)/shard_map/all_to_all | solution.py:158
  367.8 28.2 %all-to-all-start.7 = ((f32[64,4,128]{2,1,0:T(4,128)}), f32[64,4,128]{2,1,0:T(4,128)S(1)}, u32[]{:S(2)}, u32[]{:S(2)}) async-start(f32[64,4,128]{2,1,0:T(4,128)} %bitcast.40), calls=%async_computation.7 | async-start | bytes 262144 | tf_op jit(solution)/shard_map/all_to_all | solution.py:175
where the time goes:
time: 398 us; the launch traced here: 397 us
  blocking collectives  125 us (31%)
  local copies, waits for them, and re-layouts  93.1 us (23%)
  other arithmetic  63.2 us (16%)
  waiting for transfers between devices  51.9 us (13%)
  starting transfers between devices  49.4 us (12%)
  matrix products  12.9 us (3%)
    psum x1, blocking collectives, per_device(): summed = lax.psum(jnp.stack(totals), TM_AREA)  103 us
    gather x4, local copies, waits for them, and re-layouts, per_device(): gradient = unit_cost + rho_weight * jnp.take(prices, unit_bus, axis=1)  65.7 us
    scatter-add x1, other arithmetic, per_device(): injection = demand.at[:, unit_bus].add(power_time).astype(jnp.bfloat16)  44.2 us
    all_to_all x2, waiting for transfers between devices, per_device(): lax.all_to_all(power_cols, TM, split_axis=0, concat_axis=1, tiled=True)  28.2 us
    all_to_all x2, starting transfers between devices, per_device(): lax.all_to_all(target, TM, split_axis=1, concat_axis=0, tiled=True)  24.5 us
    all_to_all x2, starting transfers between devices, per_device(): lax.all_to_all(power_cols, TM, split_axis=0, concat_axis=1, tiled=True)  17.2 us
    all_to_all x2, waiting for transfers between devices, per_device(): lax.all_to_all(target, TM, split_axis=1, concat_axis=0, tiled=True)  13.5 us
    all_to_all x1, blocking collectives, copy_for_each(): lax.all_to_all(jnp.broadcast_to(array[None], (count, *array.shape)), axis...  13.3 us
  transfers between devices with their start and end apart: 6, of which 5 were waited for; matrix products, arithmetic and copies ran while one was open for 4% of the time, Pallas kernels for 0%

commit v1 on v0

--- a/solution.py
+++ b/solution.py
@@ -172,7 +172,10 @@
             preferred_element_type=jnp.float32,
         )
         power_cols = jnp.clip(smoothed, -my_cap[None, :], my_cap[None, :])
-        power_time = lax.all_to_all(power_cols, TM, split_axis=0, concat_axis=1, tiled=True)
+        power_time = jnp.concatenate(
+            lax.all_to_all(jnp.stack(jnp.split(power_cols, lax.axis_size(TM), axis=0)), TM, 0, 0),
+            axis=1,
+        )
     entries = float(horizon * line_limit.shape[0] * area_devices)
     summed = lax.psum(jnp.stack(totals), TM_AREA)
     primal_rms = jnp.sqrt(summed / entries)

time: 398 us -> 471 us (1.18)
  local copies, waits for them, and re-layouts: 93.1 us -> 167 us
    unnamed x13 -> x139, local copies, waits for them, and re-layouts: 3.99 us -> 77 us
  transfers between devices with their start and end apart: 6 -> 6, of which waited for: 5 -> 5; matrix products, arithmetic and copies ran while one was open for 4% -> 3% of each run, Pallas kernels for 0% -> 0%
where the time goes in v1:
time: 471 us; the launch traced here: 470 us
  local copies, waits for them, and re-layouts  167 us (35%)
  blocking collectives  125 us (27%)
  other arithmetic  63.2 us (13%)
  waiting for transfers between devices  51.9 us (11%)
  starting transfers between devices  49.4 us (10%)
  matrix products  11.6 us (2%)
    psum x1, blocking collectives, per_device(): summed = lax.psum(jnp.stack(totals), TM_AREA)  103 us
    unnamed x139, local copies, waits for them, and re-layouts  77 us
    gather x4, local copies, waits for them, and re-layouts, per_device(): gradient = unit_cost + rho_weight * jnp.take(prices, unit_bus, axis=1)  65.7 us
    scatter-add x1, other arithmetic, per_device(): injection = demand.at[:, unit_bus].add(power_time).astype(jnp.bfloat16)  44.2 us
    all_to_all x2, waiting for transfers between devices, per_device(): lax.all_to_all(jnp.stack(jnp.split(power_cols, lax.axis_size(TM), axis=0)...  28.2 us
    all_to_all x2, starting transfers between devices, per_device(): lax.all_to_all(target, TM, split_axis=1, concat_axis=0, tiled=True)  24.5 us
    all_to_all x2, starting transfers between devices, per_device(): lax.all_to_all(jnp.stack(jnp.split(power_cols, lax.axis_size(TM), axis=0)...  17.2 us
    all_to_all x2, waiting for transfers between devices, per_device(): lax.all_to_all(target, TM, split_axis=1, concat_axis=0, tiled=True)  13.5 us
  transfers between devices with their start and end apart: 6, of which 5 were waited for; matrix products, arithmetic and copies ran while one was open for 3% of the time, Pallas kernels for 0%

profile of v1, /device:TPU:8, one launch (start us, length us, event | category | flops | bytes accessed | tf_op | source)
XLA Modules:
  0.0 469.5 jit_solution(18356915278781812352)
XLA Ops:
  2.7 4.3 all-to-all-start
  14.3 3.5 all-to-all-done
  19.0 1.7 scatter_fusion
  22.4 3.7 scatter_fusion.1
  26.1 3.4 all-to-all-start.1
  29.5 6.7 %all-to-all-done.1 = f32[4,8,6,256]{3,0,2,1:T(4,128)S(1)} async-done(((f32[4,8,6,256]{3,0,2,1:T(4,128)}), f32[4,8,6,256]{3,0,2,1:T(4,128)S(1)}, u32[]{:S(2)}, u32[]{:S(2)}) %all-to-all-start.1) | async-done | bytes 196640 | tf_op jit(solution)/shard_map/all_to_all | solution.py:149
  36.2 2.4 scatter_fusion.2
  38.6 2.8 copy.62
  41.4 30.0 %gather_fusion.2 = f32[8192,4]{1,0:T(8,128)} fusion(f32[4,8960]{0,1:T(8,128)} %copy.62, s32[8192]{0:T(1024)S(1)} %get-tuple-element.26), kind=kCustom, calls=%fused_computation.2.clone | custom fusion | bytes 294912 | tf_op jit(solution)/shard_map/jit(_take)/gather | solution.py:156
  71.4 2.8 copy.63
  75.0 18.7 %all-to-all-start.2 = ((f32[4,64,128]{2,0,1:T(4,128)}), f32[4,64,128]{2,0,1:T(4,128)S(1)}, u32[]{:S(2)}, u32[]{:S(2)}) async-start(f32[4,64,128]{2,0,1:T(4,128)} %fusion.17), calls=%async_computation.2 | async-start | bytes 262144 | tf_op jit(solution)/shard_map/all_to_all | solution.py:158
  96.5 13.5 %all-to-all-done.2 = f32[4,64,128]{2,0,1:T(4,128)S(1)} async-done(((f32[4,64,128]{2,0,1:T(4,128)}), f32[4,64,128]{2,0,1:T(4,128)S(1)}, u32[]{:S(2)}, u32[]{:S(2)}) %all-to-all-start.2) | async-done | bytes 131104 | tf_op jit(solution)/shard_map/all_to_all | solution.py:158
  110.0 2.2 fusion.20
  112.3 1.7 fusion.1
  151.1 5.6 %all-to-all-start.3 = ((f32[64,4,128]{2,1,0:T(4,128)}), f32[64,4,128]{2,1,0:T(4,128)S(1)}, u32[]{:S(2)}, u32[]{:S(2)}) async-start(f32[64,4,128]{2,1,0:T(4,128)} %constant_dynamic-update-slice_fusion), calls=%async_computation.3 | async-start | bytes 262144 | tf_op jit(solution)/shard_map/all_to_all | solution.py:176
  156.8 2.8 copy.65
  159.6 12.8 %all-to-all-done.3 = f32[64,4,128]{2,1,0:T(4,128)S(1)} async-done(((f32[64,4,128]{2,1,0:T(4,128)}), f32[64,4,128]{2,1,0:T(4,128)S(1)}, u32[]{:S(2)}, u32[]{:S(2)}) %all-to-all-start.3) | async-done | bytes 131104 | tf_op jit(solution)/shard_map/all_to_all | solution.py:176
  172.3 2.7 copy.66
  175.0 44.2 %scatter_fusion.3 = f32[4,8960]{0,1:T(8,128)} fusion(f32[4,8960]{0,1:T(8,128)} %copy.65, s32[8192]{0:T(1024)S(1)} %get-tuple-element.25, f32[8192,4]{1,0:T(8,128)} %copy.66), kind=kCustom, calls=%fused_computation.9 | custom fusion | flops 32768 | bytes 425984 | tf_op jit(solution)/shard_map/scatter-add | solution.py:118
  219.2 3.0 copy.67
  222.4 13.3 %all_to_all.68 = bf16[8,4,8960]{2,1,0:T(4,128)(2,1)S(1)} all-to-all(bf16[8,4,8960]{2,1,0:T(4,128)(2,1)S(1)} %broadcast_in_dim.60), channel_id=1, replica_groups=mesh['tm_0'=16,'tm_1'=4,'area_0'=4,'area_1'=2] {'area_0','area_1'}, dimensions={0} | all-to-all | bytes 1146880 | tf_op jit(solution)/shard_map/all_to_all | solution.py:25
  236.8 1.7 scatter_fusion.4
  241.7 9.2 %all_to_all.69 = f32[4,8,6,256]{3,0,2,1:T(4,128)S(1)} all-to-all(f32[4,8,6,256]{3,0,2,1:T(4,128)S(1)} %bitcast.635), channel_id=1, replica_groups=mesh['tm_0'=16,'tm_1'=4,'area_0'=4,'area_1'=2] {'area_0','area_1'}, dimensions={1} | all-to-all | bytes 393216 | tf_op jit(solution)/shard_map/all_to_all | solution.py:149
  251.0 2.4 scatter_fusion.6
  253.3 2.8 copy.70
  256.1 30.0 %gather_fusion.5 = f32[8192,4]{1,0:T(8,128)} fusion(f32[4,8960]{0,1:T(8,128)} %copy.70, s32[8192]{0:T(1024)S(1)} %get-tuple-element.26), kind=kCustom, calls=%fused_computation.5.clone | custom fusion | bytes 294912 | tf_op jit(solution)/shard_map/jit(_take)/gather | solution.py:156
  286.1 2.8 copy.71
  289.7 5.8 %all-to-all-start.6 = ((f32[4,64,128]{2,0,1:T(4,128)}), f32[4,64,128]{2,0,1:T(4,128)S(1)}, u32[]{:S(2)}, u32[]{:S(2)}) async-start(f32[4,64,128]{2,0,1:T(4,128)} %fusion.14), calls=%async_computation.6 | async-start | bytes 262144 | tf_op jit(solution)/shard_map/all_to_all | solution.py:158
  296.9 102.7 %psum.7 = f32[2]{0:T(128)S(1)} all-reduce(f32[2]{0:T(128)S(1)} %pad_maximum_fusion.6), channel_id=1, replica_groups=mesh['tm_0'=16,'tm_1'=4,'area_0'=4,'area_1'=2] {'tm_0','tm_1','area_0','..., use_global_device_ids=true, to_apply=%region_12.16 | all-reduce | flops 2 | bytes 16 | tf_op jit(solution)/shard_map/psum | solution.py:180
  399.6 2.2 fusion.18
  440.7 11.6 %all-to-all-start.7 = ((f32[64,4,128]{2,1,0:T(4,128)}), f32[64,4,128]{2,1,0:T(4,128)S(1)}, u32[]{:S(2)}, u32[]{:S(2)}) async-start(f32[64,4,128]{2,1,0:T(4,128)} %constant_dynamic-update-slice_fusion.64), calls=%async_computation.7 | async-start | bytes 262144 | tf_op jit(solution)/shard_map/all_to_all | solution.py:176
  453.5 15.4 %all-to-all-done.7 = f32[64,4,128]{2,1,0:T(4,128)S(1)} async-done(((f32[64,4,128]{2,1,0:T(4,128)}), f32[64,4,128]{2,1,0:T(4,128)S(1)}, u32[]{:S(2)}, u32[]{:S(2)}) %all-to-all-start.7) | async-done | bytes 131104 | tf_op jit(solution)/shard_map/all_to_all | solution.py:176
  (204 shorter events, 100.1 us)
Async XLA Ops:
  0.6 17.8 %copy-start = (bf16[24,128,256]{2,1,0:T(8,128)(2,1)S(1)}, bf16[24,128,256]{2,1,0:T(8,128)(2,1)}, u32[]{:S(2)}) copy-start(bf16[24,128,256]{2,1,0:T(8,128)(2,1)} %param.19) | copy-start | bytes 4718596
  0.6 20.1 %copy-start.3 = (f32[1536]{0:T(1024)S(1)}, f32[1536]{0:T(1024)}, u32[]{:S(2)}) copy-start(f32[1536]{0:T(1024)} %param.26) | copy-start | bytes 18436
  2.7 15.1 %all-to-all-start = ((bf16[8,4,8960]{2,1,0:T(4,128)(2,1)}), bf16[8,4,8960]{2,1,0:T(4,128)(2,1)S(1)}, u32[]{:S(2)}, u32[]{:S(2)}) async-start(bf16[8,4,8960]{2,1,0:T(4,128)(2,1)} %broadcast_in_dim.55), calls=%async_computation | async-start | bytes 1146880 | tf_op jit(solution)/shard_map/all_to_all | solution.py:25
  26.1 10.1 %all-to-all-start.1 = ((f32[4,8,6,256]{3,0,2,1:T(4,128)}), f32[4,8,6,256]{3,0,2,1:T(4,128)S(1)}, u32[]{:S(2)}, u32[]{:S(2)}) async-start(f32[4,8,6,256]{3,0,2,1:T(4,128)} %bitcast.15), calls=%async_computation.1 | async-start | bytes 393216 | tf_op jit(solution)/shard_map/all_to_all | solution.py:149
  38.6 35.7 %copy-start.2 = (f32[4,8192]{1,0:T(4,128)S(1)}, f32[4,8192]{1,0:T(4,128)}, u32[]{:S(2)}) copy-start(f32[4,8192]{1,0:T(4,128)} %param.18) | copy-start | bytes 393220
  41.4 52.3 %copy-start.4 = (f32[3,256]{1,0:T(4,128)S(1)}, f32[3,256]{1,0:T(4,128)}, u32[]{:S(2)}) copy-start(f32[3,256]{1,0:T(4,128)} %param.27) | copy-start | bytes 9220
  74.3 82.5 %copy-start.1 = (f32[4,8960]{1,0:T(4,128)S(1)}, f32[4,8960]{1,0:T(4,128)}, u32[]{:S(2)}) copy-start(f32[4,8960]{1,0:T(4,128)} %param.17) | copy-start | bytes 430084
  75.0 35.0 %all-to-all-start.2 = ((f32[4,64,128]{2,0,1:T(4,128)}), f32[4,64,128]{2,0,1:T(4,128)S(1)}, u32[]{:S(2)}, u32[]{:S(2)}) async-start(f32[4,64,128]{2,0,1:T(4,128)} %fusion.17), calls=%async_computation.2 | async-start | bytes 262144 | tf_op jit(solution)/shard_map/all_to_all | solution.py:158
  151.1 21.2 %all-to-all-start.3 = ((f32[64,4,128]{2,1,0:T(4,128)}), f32[64,4,128]{2,1,0:T(4,128)S(1)}, u32[]{:S(2)}, u32[]{:S(2)}) async-start(f32[64,4,128]{2,1,0:T(4,128)} %constant_dynamic-update-slice_fusion), calls=%async_computation.3 | async-start | bytes 262144 | tf_op jit(solution)/shard_map/all_to_all | solution.py:176
  289.7 109.9 %all-to-all-start.6 = ((f32[4,64,128]{2,0,1:T(4,128)}), f32[4,64,128]{2,0,1:T(4,128)S(1)}, u32[]{:S(2)}, u32[]{:S(2)}) async-start(f32[4,64,128]{2,0,1:T(4,128)} %fusion.14), calls=%async_computation.6 | async-start | bytes 262144 | tf_op jit(solution)/shard_map/all_to_all | solution.py:158
  440.7 28.2 %all-to-all-start.7 = ((f32[64,4,128]{2,1,0:T(4,128)}), f32[64,4,128]{2,1,0:T(4,128)S(1)}, u32[]{:S(2)}, u32[]{:S(2)}) async-start(f32[64,4,128]{2,1,0:T(4,128)} %constant_dynamic-update-slice_fusion.64), calls=%async_computation.7 | async-start | bytes 262144 | tf_op jit(solution)/shard_map/all_to_all | solution.py:176
